TPU v7x, 128 devices: a whole 4x4x4 slice. The times are simulated.
128 devices in a mesh: sec: 2 (over x_hi), head: 4 (over x_lo, core), ctx: 16 (over z, y).
Axes of the slice: x: 4 (x_hi: 2, x_lo: 2; x = x_hi * 2 + x_lo), y: 4, z: 4, core: 2. Of those that a mesh axis runs over, the one named last changes fastest.
Arguments:
- proposal_rows: bfloat16 [512, 8192], P('sec', 'ctx'), may hold values from -400 to 400
- norm_gain: bfloat16 [8192], P('ctx'), may hold values from 0.25 to 1.75
- query_weight: bfloat16 [8192, 8192], P('ctx', ('sec', 'head')), may hold values from -0.0625 to 0.0625
- key_weight: bfloat16 [8192, 8, 128], P('ctx', ('sec', 'head')), may hold values from -0.25 to 0.25
- value_weight: bfloat16 [8192, 8, 128], P('ctx', ('sec', 'head')), may hold values from -0.0625 to 0.0625
- out_weight: bfloat16 [8192, 8192], P(('sec', 'head'), 'ctx'), may hold values from -0.0625 to 0.0625
- context_keys: bfloat16 [32768, 8, 128], P('ctx', ('sec', 'head')), may hold values from -256 to 256
- context_values: bfloat16 [32768, 8, 128], P('ctx', ('sec', 'head')), may hold values from -5 to 5
- prefix_lengths: int32 [32], replicated, may hold values from 2048 to 32768, as said below
- parents: int32 [512], replicated, may hold values from -1 to 510, as said below
Outputs:
- block_output: bfloat16 [512, 8192], P(('sec', 'head'), 'ctx')
Inputs may be any that keep to these rules, and one draw needn't show every extreme that they name: `parents`: token i = 16 p + s of particle p has parent -1 when s = 0, else 16 q + s - 1 for some particle q <= p. `prefix_lengths`: some particle sees the whole context.
All inputs are finite; a program needn't handle non-finite values.
Results may differ from a plain program's by a relative error of at most 0.015.
The roundings to bfloat16 on the way count: a program that leaves them out, or rounds other values in their place, can miss the bound.
Values may be sent and summed in bfloat16 or wider, within the bound.
No kernel may reach another device: no remote copies, remote signals or barrier semaphores. Data moves between devices by JAX's collectives and lax.ppermute only.
A program may use at most 192 MiB of HBM per device.

v0:
```python
import math
import jax
import jax.numpy as jnp
from jax import lax
from jax.sharding import PartitionSpec as P

D = 8192
PROPOSALS = 16
NEGATIVE = -1e30
EPSILON = 1e-05


def ancestry_columns(parents, column_offset, column_amount):
    total = parents.shape[0]
    index = jnp.arange(total, dtype=jnp.int32)
    step = jnp.logical_or(parents[:, None] == index[None, :], index[:, None] == index[None, :])
    reach = step.astype(jnp.bfloat16)
    for _ in range(3):
        reach = (jnp.dot(reach, reach, preferred_element_type=jnp.float32) > 0).astype(jnp.bfloat16)
    columns = lax.dynamic_slice_in_dim(reach, column_offset, column_amount, 1)
    return jnp.dot(reach, columns, preferred_element_type=jnp.float32) > 0


def body(
    proposal_rows,
    norm_gain,
    query_weight,
    key_weight,
    value_weight,
    out_weight,
    context_keys,
    context_values,
    prefix_lengths,
    parents,
):
    gathered = lax.all_gather(proposal_rows, "sec", axis=0, tiled=True)
    gathered_wide = gathered.astype(jnp.float32)
    total_rows = gathered.shape[0]
    squares = jnp.sum(gathered_wide * gathered_wide, axis=1)
    scaled = (gathered_wide * norm_gain.astype(jnp.float32)[None, :]).astype(jnp.bfloat16)
    query_width = query_weight.shape[1]
    head_size = key_weight.shape[2]
    groups = query_width // head_size
    joined = jnp.concatenate([query_weight, key_weight[:, 0, :], value_weight[:, 0, :]], axis=1)
    partial_value = jnp.dot(scaled, joined, preferred_element_type=jnp.float32)
    proj_width = partial_value.shape[1]
    lane = jnp.arange(128, dtype=jnp.int32)
    square_block = jnp.where(lane[None, :] == 0, squares[:, None], 0.0)
    packed = jnp.concatenate([partial_value, square_block], axis=1)
    reduced = lax.psum_scatter(packed, "ctx", scatter_dimension=0, tiled=True)
    row_share = reduced.shape[0]
    inverse = lax.rsqrt(reduced[:, proj_width] / D + EPSILON)[:, None]
    settled = reduced[:, :proj_width] * inverse
    own_queries = settled[:, :query_width].astype(jnp.bfloat16)
    tree_keys = settled[:, query_width : query_width + head_size].astype(jnp.bfloat16)
    tree_vals = settled[:, query_width + head_size :].astype(jnp.bfloat16)
    queries = lax.all_gather(own_queries, "ctx", axis=0, tiled=True)
    position = lax.axis_index("ctx")
    keys = context_keys[:, 0, :]
    vals = context_values[:, 0, :]
    span = keys.shape[0]
    factor = 1.0 / math.sqrt(head_size)
    grouped = queries.reshape(total_rows, groups, head_size)
    lengths_rows = jnp.repeat(prefix_lengths, PROPOSALS)
    positions = position * span + jnp.arange(span, dtype=jnp.int32)
    visible = (positions[None, :] < lengths_rows[:, None])[:, None, :]
    scores = jnp.einsum("rgd,td->rgt", grouped, keys, preferred_element_type=jnp.float32) * factor
    tree_visible = ancestry_columns(parents, position * row_share, row_share)[:, None, :]
    tree_scores = (
        jnp.einsum("rgd,td->rgt", grouped, tree_keys, preferred_element_type=jnp.float32) * factor
    )
    local_high = jnp.maximum(
        jnp.max(jnp.where(visible, scores, NEGATIVE), axis=2),
        jnp.max(jnp.where(tree_visible, tree_scores, NEGATIVE), axis=2),
    )
    highest = lax.pmax(local_high, "ctx")
    weights = jnp.where(visible, jnp.exp(scores - highest[:, :, None]), 0.0)
    tree_weights = jnp.where(tree_visible, jnp.exp(tree_scores - highest[:, :, None]), 0.0)
    weight_sum = jnp.sum(weights, axis=2) + jnp.sum(tree_weights, axis=2)
    summed = jnp.einsum(
        "rgt,td->rgd", weights.astype(jnp.bfloat16), vals, preferred_element_type=jnp.float32
    ) + jnp.einsum(
        "rgt,td->rgd",
        tree_weights.astype(jnp.bfloat16),
        tree_vals,
        preferred_element_type=jnp.float32,
    )
    sum_block = jnp.concatenate(
        [weight_sum, jnp.zeros((total_rows, 128 - groups), jnp.float32)], axis=1
    )
    packed_attn = jnp.concatenate([summed.reshape(total_rows, query_width), sum_block], axis=1)
    merged = lax.psum_scatter(packed_attn, "ctx", scatter_dimension=0, tiled=True)
    own_attended = (
        (
            merged[:, :query_width].reshape(row_share, groups, head_size)
            / merged[:, query_width : query_width + groups][:, :, None]
        )
        .reshape(row_share, query_width)
        .astype(jnp.bfloat16)
    )
    attended = lax.all_gather(own_attended, "ctx", axis=0, tiled=True)
    return lax.psum_scatter(
        jnp.dot(attended, out_weight, preferred_element_type=jnp.float32).astype(jnp.bfloat16),
        ("sec", "head"),
        scatter_dimension=0,
        tiled=True,
    )


def solution(mesh):
    placed = (
        P("sec", "ctx"),
        P("ctx"),
        P("ctx", ("sec", "head")),
        P("ctx", ("sec", "head"), None),
        P("ctx", ("sec", "head"), None),
        P(("sec", "head"), "ctx"),
        P("ctx", ("sec", "head"), None),
        P("ctx", ("sec", "head"), None),
        P(),
        P(),
    )
    return jax.shard_map(
        body, mesh=mesh, in_specs=placed, out_specs=P(("sec", "head"), "ctx"), check_vma=False
    )
```

profile of v0, /device:TPU:0, one launch (start us, length us, event | category | flops | bytes accessed | tf_op | source)
XLA Modules:
  0.0 426.5 jit_solution(10706751456148544928)
XLA Ops:
  6.5 10.5 %all_gather.9 = bf16[512,512]{1,0:T(8,128)(2,1)S(1)} all-gather(bf16[256,512]{1,0:T(8,128)(2,1)} %param.10), channel_id=1, replica_groups=mesh['sec'=2,'head'=4,'ctx'=16] {'sec'}, dimensions={0}, use_global_device_ids=true | all-gather | bytes 786432 | tf_op jit(solution)/shard_map/all_gather | solution.py:36
  17.0 0.7 convert_element_type.29
  18.0 2.2 fusion.5
  20.3 1.8 pad_maximum_fusion
  22.1 79.1 %reduce-scatter.6.cloned.1.call-done = f32[32,1408]{1,0:T(8,128)} async-done(((f32[512,1408]{1,0:T(8,128)}), f32[32,1408]{1,0:T(8,128)}) %reduce-scatter.6.cloned.1.call-update) | async-done | bytes 180240 | tf_op jit(solution)/shard_map/reduce_scatter | solution.py:50
  101.3 0.8 fusion.37
  102.1 1.0 fusion.34
  104.7 1.1 convolution_compare_fusion
  106.3 0.7 broadcast_compare_fusion
  106.9 38.8 %all-gather.3.cloned.1.call-done = bf16[512,1024]{1,0:T(8,128)(2,1)} async-done(((bf16[32,1024]{1,0:T(8,128)(2,1)}), bf16[512,1024]{1,0:T(8,128)(2,1)}) %all-gather.3.cloned.1.call-update) | async-done | bytes 1048592 | tf_op jit(solution)/shard_map/all_gather | solution.py:57
  145.7 1.7 select_reduce_fusion.1
  147.4 15.1 %select_reduce_fusion = (f32[512,8]{0,1:T(8,128)S(1)}, f32[512,8,2048]{2,0,1:T(8,128)}) fusion(pred[512,2048]{1,0:T(8,128)(4,1)S(1)} %broadcast_compare_fusion, bf16[2048,1,128]{2,0,1:T(8,128)(2,1)S(1)} %copy-done.1, bf16[512,1024]{1,0:T(8,128)(2,1)} %all-gather.3.cloned.1.call-done), kind=kOutput, calls=%fused_computation.1 | convolution fusion | flops 2172645376 | bytes 36192256 | tf_op jit(solution)/shard_map/rgd,td->rgt/dot_general | solution.py:67
  162.5 72.1 %pmax.7 = f32[512,8]{0,1:T(8,128)S(1)} all-reduce(f32[512,8]{0,1:T(8,128)S(1)} %max.5), channel_id=1, replica_groups=mesh['sec'=2,'head'=4,'ctx'=16] {'ctx'}, use_global_device_ids=true, to_apply=%region_4.5 | all-reduce | flops 4096 | bytes 32768 | tf_op jit(solution)/shard_map/pmax | solution.py:76
  234.6 15.2 %fusion = f32[512,8]{0,1:T(8,128)S(1)} fusion(f32[512,8,2048]{2,0,1:T(8,128)} %get-tuple-element.6, f32[512,8]{0,1:T(8,128)S(1)} %pmax.7, pred[512,2048]{1,0:T(8,128)(4,1)S(1)} %broadcast_compare_fusion), kind=kLoop, calls=%fused_computation.2 | loop fusion | flops 33550336 | bytes 34635776 | tf_op jit(solution)/shard_map/reduce_sum | solution.py:79
  249.8 15.4 %fusion.2 = f32[512,8,128]{0,2,1:T(8,128)} fusion(f32[512,8,2048]{2,0,1:T(8,128)} %get-tuple-element.6, f32[512,8]{0,1:T(8,128)S(1)} %pmax.7, pred[512,2048]{1,0:T(8,128)(4,1)S(1)} %broadcast_compare_fusion, bf16[2048,1,128]{2,0,1:T(8,128)(2,1)} %param.17), kind=kOutput, calls=%fused_computation.4 | convolution fusion | flops 2181038080 | bytes 37240832 | tf_op jit(solution)/shard_map/rgt,td->rgd/dot_general | solution.py:80
  265.3 2.1 convolution_add_fusion
  267.7 2.0 copy.25
  269.7 72.2 %reduce-scatter.10.cloned.1.call-done = f32[32,1152]{1,0:T(8,128)} async-done(((f32[512,1152]{1,0:T(8,128)}), f32[32,1152]{1,0:T(8,128)}) %reduce-scatter.10.cloned.1.call-update) | async-done | bytes 147472
  341.9 0.9 slice.36
  343.0 0.7 slice.37
  343.8 0.8 copy.21
  344.7 42.0 %all-gather.5.cloned.1.call-done = bf16[512,1024]{1,0:T(8,128)(2,1)} async-done(((bf16[32,1024]{1,0:T(8,128)(2,1)}), bf16[512,1024]{1,0:T(8,128)(2,1)}) %all-gather.5.cloned.1.call-update) | async-done | bytes 1048592 | tf_op jit(solution)/shard_map/all_gather | solution.py:101
  386.6 2.8 convolution_convert_fusion
  389.4 30.6 %reduce-scatter.8.cloned.1.call-done = bf16[64,512]{1,0:T(8,128)(2,1)} async-done(((bf16[512,512]{1,0:T(8,128)(2,1)}), bf16[64,512]{1,0:T(8,128)(2,1)}) %reduce-scatter.8.cloned.1.call-update) | async-done | bytes 65552 | tf_op jit(solution)/shard_map/reduce_scatter | solution.py:102
  (36 shorter events, 3.2 us)
Async XLA Ops:
  6.5 380.1 %copy-start = (bf16[1024,512]{1,0:T(8,128)(2,1)S(1)}, bf16[1024,512]{1,0:T(8,128)(2,1)}, u32[]{:S(2)}) copy-start(bf16[1024,512]{1,0:T(8,128)(2,1)} %param.15) | copy-start | bytes 3145732
  6.5 94.7 %reduce-scatter.6.cloned.1.call-start = ((), (), s32[]{:S(2)}) async-start(), calls=%async_computation.3 | async-start | bytes 3063808 | tf_op jit(solution)/shard_map/reduce_scatter | solution.py:50
  22.1 81.8 %copy-start.2 = (s32[32]{0:T(128)S(1)}, s32[32]{0:T(128)}, u32[]{:S(2)}) copy-start(s32[32]{0:T(128)} %param.18) | copy-start | bytes 388
  22.1 82.0 %copy-start.3 = (s32[512]{0:T(512)S(1)}, s32[512]{0:T(512)}, u32[]{:S(2)}) copy-start(s32[512]{0:T(512)} %param.19) | copy-start | bytes 6148
  22.1 123.6 %all-gather.3.cloned.1.call-start = ((), (), s32[]{:S(2)}) async-start(), calls=%async_computation.4 | async-start | bytes 1114112 | tf_op jit(solution)/shard_map/all_gather | solution.py:57
  103.8 238.1 %reduce-scatter.10.cloned.1.call-start = ((), (), s32[]{:S(2)}) async-start(), calls=%async_computation.7 | async-start | bytes 2506752
  104.7 42.7 %copy-start.1 = (bf16[2048,1,128]{2,0,1:T(8,128)(2,1)S(1)}, bf16[2048,1,128]{2,0,1:T(8,128)(2,1)}, u32[]{:S(2)}) copy-start(bf16[2048,1,128]{2,0,1:T(8,128)(2,1)} %param.16) | copy-start | bytes 1572868
  269.7 117.0 %all-gather.5.cloned.1.call-start = ((), (), s32[]{:S(2)}) async-start(), calls=%async_computation.5 | async-start | bytes 1114112 | tf_op jit(solution)/shard_map/all_gather | solution.py:101
  344.6 75.4 %reduce-scatter.8.cloned.1.call-start = ((), (), s32[]{:S(2)}) async-start(), calls=%async_computation.6 | async-start | bytes 589824 | tf_op jit(solution)/shard_map/reduce_scatter | solution.py:102
Sparse Core Ops, SparseCore 0:
  22.2 79.0 reduce-scatter.5
  103.9 41.7 all-gather.2
  269.8 72.0 reduce-scatter.9
  344.7 41.8 all-gather.4
  389.5 30.4 reduce-scatter.7
where the time goes:
time: 427 us
  waiting for transfers between devices  263 us (62%)
  blocking collectives  82.6 us (19%)
  matrix products  41.4 us (10%)
  other arithmetic  20.8 us (5%)
  between operations  13.3 us (3%)
  local copies, waits for them, and re-layouts  5.52 us (1%)
    reduce_scatter x1, waiting for transfers between devices, body(): reduced = lax.psum_scatter(packed, 'ctx', scatter_dimension=0, tiled=True)  79.1 us
    unnamed x6, waiting for transfers between devices  72.2 us
    pmax x1, blocking collectives, body(): highest = lax.pmax(local_high, 'ctx')  72.1 us
    all_gather x1, waiting for transfers between devices, body(): attended = lax.all_gather(own_attended, 'ctx', axis=0, tiled=True)  42 us
    all_gather x1, waiting for transfers between devices, body(): queries = lax.all_gather(own_queries, 'ctx', axis=0, tiled=True)  38.8 us
    reduce_scatter x1, waiting for transfers between devices, body(): lax.psum_scatter(jnp.dot(attended, out_weight, preferred_element_type=jnp...  30.6 us
    dot_general x1, matrix products, body(): jnp.einsum('rgt,td->rgd', weights.astype(jnp.bfloat16), vals, preferred_e...  15.4 us
    reduce_sum x2, other arithmetic, body(): weight_sum = jnp.sum(weights, axis=2) + jnp.sum(tree_weights, axis=2)  15.3 us
  transfers between devices with their start and end apart: 5, of which 5 were waited for; matrix products, arithmetic and copies ran while one was open for 1% of the time, Pallas kernels for 0%

commit v1 on v0

--- a/solution.py
+++ b/solution.py
@@ -54,7 +54,9 @@
     own_queries = settled[:, :query_width].astype(jnp.bfloat16)
     tree_keys = settled[:, query_width : query_width + head_size].astype(jnp.bfloat16)
     tree_vals = settled[:, query_width + head_size :].astype(jnp.bfloat16)
-    queries = lax.all_gather(own_queries, "ctx", axis=0, tiled=True)
+    queries = jnp.concatenate(
+        lax.all_to_all(jnp.stack([own_queries] * lax.axis_size("ctx")), "ctx", 0, 0), axis=0
+    )
     position = lax.axis_index("ctx")
     keys = context_keys[:, 0, :]
     vals = context_values[:, 0, :]

time: 427 us -> 403 us (0.944)
  waiting for transfers between devices: 263 us -> 237 us
  starting transfers between devices: 0.17 us -> 5.02 us
    all_gather x1 -> x0, waiting for transfers between devices: 38.8 us -> none  [body(): queries = lax.all_gather(own_queries, 'ctx', axis=0, tiled=True)]
    all_to_all x0 -> x1, waiting for transfers between devices: none -> 12.5 us  [body(): lax.all_to_all(jnp.stack([own_queries] * lax.axis_size('ctx')), 'ctx', 0, 0)]
    all_to_all x0 -> x1, starting transfers between devices: none -> 4.89 us  [body(): lax.all_to_all(jnp.stack([own_queries] * lax.axis_size('ctx')), 'ctx', 0, 0)]
    unnamed x6 -> x5, waiting for transfers between devices: 72.2 us -> 72.3 us
where the time goes in v1:
time: 403 us; the launch traced here: 402 us
  waiting for transfers between devices  237 us (59%)
  blocking collectives  80.9 us (20%)
  matrix products  39.1 us (10%)
  other arithmetic  20.8 us (5%)
  between operations  13.3 us (3%)
  local copies, waits for them, and re-layouts  6.53 us (2%)
  starting transfers between devices  5.02 us (1%)
    reduce_scatter x1, waiting for transfers between devices, body(): reduced = lax.psum_scatter(packed, 'ctx', scatter_dimension=0, tiled=True)  79.2 us
    unnamed x5, waiting for transfers between devices  72.3 us
    pmax x1, blocking collectives, body(): highest = lax.pmax(local_high, 'ctx')  70.4 us
    all_gather x1, waiting for transfers between devices, body(): attended = lax.all_gather(own_attended, 'ctx', axis=0, tiled=True)  41.9 us
    reduce_scatter x1, waiting for transfers between devices, body(): lax.psum_scatter(jnp.dot(attended, out_weight, preferred_element_type=jnp...  30.6 us
    dot_general x1, matrix products, body(): jnp.einsum('rgt,td->rgd', weights.astype(jnp.bfloat16), vals, preferred_e...  15.4 us
    reduce_sum x2, other arithmetic, body(): weight_sum = jnp.sum(weights, axis=2) + jnp.sum(tree_weights, axis=2)  15.3 us
    dot_general x1, matrix products, body(): jnp.einsum('rgd,td->rgt', grouped, keys, preferred_element_type=jnp.float32)  13.9 us
  transfers between devices with their start and end apart: 5, of which 5 were waited for; matrix products, arithmetic and copies ran while one was open for 1% of the time, Pallas kernels for 0%

profile of v1, /device:TPU:0, one launch (start us, length us, event | category | flops | bytes accessed | tf_op | source)
XLA Modules:
  0.0 402.2 jit_solution(12428744652340282152)
XLA Ops:
  6.5 10.5 %all_gather.6 = bf16[512,512]{1,0:T(8,128)(2,1)S(1)} all-gather(bf16[256,512]{1,0:T(8,128)(2,1)} %param.10), channel_id=1, replica_groups=mesh['sec'=2,'head'=4,'ctx'=16] {'sec'}, dimensions={0}, use_global_device_ids=true | all-gather | bytes 786432 | tf_op jit(solution)/shard_map/all_gather | solution.py:36
  17.0 0.7 convert_element_type.29
  18.0 2.2 fusion.5
  20.3 1.8 pad_maximum_fusion
  22.1 79.2 %reduce-scatter.6.cloned.1.call-done = f32[32,1408]{1,0:T(8,128)} async-done(((f32[512,1408]{1,0:T(8,128)}), f32[32,1408]{1,0:T(8,128)}) %reduce-scatter.6.cloned.1.call-update) | async-done | bytes 180240 | tf_op jit(solution)/shard_map/reduce_scatter | solution.py:50
  101.3 0.8 fusion.35
  102.1 1.0 fusion.32
  103.1 1.1 stack.2
  104.2 4.9 %all-to-all-start = ((bf16[16,32,1024]{2,1,0:T(8,128)(2,1)}), bf16[16,32,1024]{2,1,0:T(8,128)(2,1)S(1)}, u32[]{:S(2)}, u32[]{:S(2)}) async-start(bf16[16,32,1024]{2,1,0:T(8,128)(2,1)} %stack.2), calls=%async_computation.1 | async-start | bytes 2097152 | tf_op jit(solution)/shard_map/all_to_all | solution.py:58
  110.1 1.1 convolution_compare_fusion
  112.3 12.5 %all-to-all-done = bf16[16,32,1024]{2,1,0:T(8,128)(2,1)S(1)} async-done(((bf16[16,32,1024]{2,1,0:T(8,128)(2,1)}), bf16[16,32,1024]{2,1,0:T(8,128)(2,1)S(1)}, u32[]{:S(2)}, u32[]{:S(2)}) %all-to-all-start) | async-done | bytes 1048608 | tf_op jit(solution)/shard_map/all_to_all | solution.py:58
  125.8 13.9 %select_reduce_fusion = (f32[512,8]{0,1:T(8,128)S(1)}, f32[512,8,2048]{2,0,1:T(8,128)}) fusion(pred[512,2048]{1,0:T(8,128)(4,1)S(1)} %broadcast_compare_fusion, bf16[2048,1,128]{2,0,1:T(8,128)(2,1)S(1)} %copy-done.1, bf16[512,8,128]{2,1,0:T(8,128)(2,1)S(1)} %bitcast.37), kind=kOutput, calls=%fused_computation.1 | convolution fusion | flops 2172645376 | bytes 36192256 | tf_op jit(solution)/shard_map/rgd,td->rgt/dot_general | solution.py:69
  139.8 70.4 %pmax.7 = f32[512,8]{0,1:T(8,128)S(1)} all-reduce(f32[512,8]{0,1:T(8,128)S(1)} %max.5), channel_id=1, replica_groups=mesh['sec'=2,'head'=4,'ctx'=16] {'ctx'}, use_global_device_ids=true, to_apply=%region_4.5 | all-reduce | flops 4096 | bytes 32768 | tf_op jit(solution)/shard_map/pmax | solution.py:78
  210.1 15.2 %fusion = f32[512,8]{0,1:T(8,128)S(1)} fusion(f32[512,8,2048]{2,0,1:T(8,128)} %get-tuple-element.6, f32[512,8]{0,1:T(8,128)S(1)} %pmax.7, pred[512,2048]{1,0:T(8,128)(4,1)S(1)} %broadcast_compare_fusion), kind=kLoop, calls=%fused_computation.2 | loop fusion | flops 33550336 | bytes 34635776 | tf_op jit(solution)/shard_map/reduce_sum | solution.py:81
  225.3 15.4 %fusion.2 = f32[512,8,128]{0,2,1:T(8,128)} fusion(f32[512,8,2048]{2,0,1:T(8,128)} %get-tuple-element.6, f32[512,8]{0,1:T(8,128)S(1)} %pmax.7, pred[512,2048]{1,0:T(8,128)(4,1)S(1)} %broadcast_compare_fusion, bf16[2048,1,128]{2,0,1:T(8,128)(2,1)} %param.17), kind=kOutput, calls=%fused_computation.4 | convolution fusion | flops 2181038080 | bytes 37240832 | tf_op jit(solution)/shard_map/rgt,td->rgd/dot_general | solution.py:82
  240.9 2.1 convolution_add_fusion
  243.2 2.0 copy.23
  245.3 72.2 %reduce-scatter.10.cloned.1.call-done = f32[32,1152]{1,0:T(8,128)} async-done(((f32[512,1152]{1,0:T(8,128)}), f32[32,1152]{1,0:T(8,128)}) %reduce-scatter.10.cloned.1.call-update) | async-done | bytes 147472
  317.5 0.9 slice.36
  318.6 0.7 slice.37
  319.5 0.8 copy.19
  320.3 41.9 %all-gather.2.cloned.1.call-done = bf16[512,1024]{1,0:T(8,128)(2,1)} async-done(((bf16[32,1024]{1,0:T(8,128)(2,1)}), bf16[512,1024]{1,0:T(8,128)(2,1)}) %all-gather.2.cloned.1.call-update) | async-done | bytes 1048592 | tf_op jit(solution)/shard_map/all_gather | solution.py:103
  362.2 2.8 convolution_convert_fusion
  365.0 30.6 %reduce-scatter.8.cloned.1.call-done = bf16[64,512]{1,0:T(8,128)(2,1)} async-done(((bf16[512,512]{1,0:T(8,128)(2,1)}), bf16[64,512]{1,0:T(8,128)(2,1)}) %reduce-scatter.8.cloned.1.call-update) | async-done | bytes 65552 | tf_op jit(solution)/shard_map/reduce_scatter | solution.py:104
  (37 shorter events, 4.1 us)
Async XLA Ops:
  6.5 355.7 %copy-start = (bf16[1024,512]{1,0:T(8,128)(2,1)S(1)}, bf16[1024,512]{1,0:T(8,128)(2,1)}, u32[]{:S(2)}) copy-start(bf16[1024,512]{1,0:T(8,128)(2,1)} %param.15) | copy-start | bytes 3145732
  6.5 94.7 %reduce-scatter.6.cloned.1.call-start = ((), (), s32[]{:S(2)}) async-start(), calls=%async_computation.4 | async-start | bytes 3063808 | tf_op jit(solution)/shard_map/reduce_scatter | solution.py:50
  22.1 87.2 %copy-start.2 = (s32[32]{0:T(128)S(1)}, s32[32]{0:T(128)}, u32[]{:S(2)}) copy-start(s32[32]{0:T(128)} %param.18) | copy-start | bytes 388
  22.1 87.4 %copy-start.3 = (s32[512]{0:T(512)S(1)}, s32[512]{0:T(512)}, u32[]{:S(2)}) copy-start(s32[512]{0:T(512)} %param.19) | copy-start | bytes 6148
  104.2 20.6 %all-to-all-start = ((bf16[16,32,1024]{2,1,0:T(8,128)(2,1)}), bf16[16,32,1024]{2,1,0:T(8,128)(2,1)S(1)}, u32[]{:S(2)}, u32[]{:S(2)}) async-start(bf16[16,32,1024]{2,1,0:T(8,128)(2,1)} %stack.2), calls=%async_computation.1 | async-start | bytes 2097152 | tf_op jit(solution)/shard_map/all_to_all | solution.py:58
  109.1 208.4 %reduce-scatter.10.cloned.1.call-start = ((), (), s32[]{:S(2)}) async-start(), calls=%async_computation.7 | async-start | bytes 2506752
  124.8 1.0 copy-start.1
  245.2 117.0 %all-gather.2.cloned.1.call-start = ((), (), s32[]{:S(2)}) async-start(), calls=%async_computation.5 | async-start | bytes 1114112 | tf_op jit(solution)/shard_map/all_gather | solution.py:103
  320.3 75.4 %reduce-scatter.8.cloned.1.call-start = ((), (), s32[]{:S(2)}) async-start(), calls=%async_computation.6 | async-start | bytes 589824 | tf_op jit(solution)/shard_map/reduce_scatter | solution.py:104
Sparse Core Ops, SparseCore 0:
  22.2 79.0 reduce-scatter.5
  245.3 72.1 reduce-scatter.9
  320.4 41.8 all-gather.1
  365.1 30.4 reduce-scatter.7
